TPU v7x, 32 devices: a whole 2x2x4 slice. The times are simulated.
32 devices in a mesh: rows: 4 (over x, core), dp: 8 (over z, y).
Axes of the slice: x: 2, y: 2, z: 4, core: 2. Of those that a mesh axis runs over, the one named last changes fastest.
Arguments:
- latents: bfloat16 [8, 8, 128, 640], P('dp', 'rows'), may hold values from -160 to 160
- timesteps: int32 [8], P('dp'), may hold values from 0 to 999
- gn_gain: float32 [640], replicated, may hold values from 0.1 to 1.9
- gn_bias: float32 [640], replicated, may hold values from -3 to 3
- conv_weight: bfloat16 [3, 3, 640, 640], replicated, may hold values from -0.078125 to 0.078125
- conv_bias: float32 [640], replicated, may hold values from -3 to 3
- temb_weight: bfloat16 [1280, 640], replicated, may hold values from -0.25 to 0.25
- cotangent: bfloat16 [8, 8, 128, 640], P('dp', 'rows'), may hold values from -6 to 6
Outputs:
- features_out: bfloat16 [8, 8, 128, 640], P('dp', 'rows')
- input_grad: bfloat16 [8, 8, 128, 640], P('dp', 'rows')
- norm_grads: float32 [3, 640], replicated
All inputs are finite; a program needn't handle non-finite values.
Results may differ from a plain program's by a relative error of at most 0.0044.
Values may be sent and summed in bfloat16 or wider, within the bound.
No kernel may reach another device: no remote copies, remote signals or barrier semaphores. Data moves between devices by JAX's collectives and lax.ppermute only.
A program may use at most 64 MiB of HBM per device.

v0:
```python
import math
import jax
import jax.numpy as jnp
from jax import lax
from jax.sharding import PartitionSpec as P

CH_GROUP = 40
NORM_EPS = 1e-05


def padded_2(cells, sides, width):
    for axis, dim in sides:
        count = lax.axis_size(axis)
        ends = count - 1
        head = lax.slice_in_dim(cells, 0, width, axis=dim)
        tail = lax.slice_in_dim(cells, cells.shape[dim] - width, cells.shape[dim], axis=dim)
        cells = jnp.concatenate(
            [
                lax.ppermute(tail, axis, [(i, (i + 1) % count) for i in range(ends)]),
                cells,
                lax.ppermute(head, axis, [((i + 1) % count, i) for i in range(ends)]),
            ],
            axis=dim,
        )
    return cells


def sinusoid(steps, embed_dim):
    half_dim = embed_dim // 2
    frequencies = jnp.exp(-math.log(10000.0) * jnp.arange(half_dim).astype(jnp.float32) / half_dim)
    angles = steps.astype(jnp.float32)[:, None] * frequencies[None, :]
    return jnp.concatenate([jnp.cos(angles), jnp.sin(angles)], axis=1)


def with_rim(field):
    return padded_2(field, (("rows", 1),), 1)


def conv_taps(extended, weight, slab_rows, col_count, backward):
    padded = jnp.pad(extended, ((0, 0), (0, 0), (1, 1), (0, 0)))
    images = padded.shape[0]
    channels = padded.shape[3]
    total = None
    for tap_row in range(3):
        for tap_col in range(3):
            if backward:
                row_start, col_start = (2 - tap_row, 2 - tap_col)
            else:
                row_start, col_start = (tap_row, tap_col)
            window = padded[
                :, row_start : row_start + slab_rows, col_start : col_start + col_count
            ].reshape(-1, channels)
            if backward:
                tap_term = lax.dot_general(
                    window,
                    weight[tap_row, tap_col],
                    (((1,), (1,)), ((), ())),
                    preferred_element_type=jnp.float32,
                )
            else:
                tap_term = jnp.dot(
                    window, weight[tap_row, tap_col], preferred_element_type=jnp.float32
                )
            total = tap_term if total is None else total + tap_term
    return total.reshape(images, slab_rows, col_count, -1)


def per_device(
    latents, timesteps, gn_gain, gn_bias, conv_weight, conv_bias, temb_weight, cotangent
):
    images, slab_rows, col_count, channels = latents.shape
    groups = channels // CH_GROUP
    row_devices = lax.axis_size("rows")
    group_cells = slab_rows * row_devices * col_count * CH_GROUP
    grouped = latents.astype(jnp.float32).reshape(images, slab_rows, col_count, groups, CH_GROUP)
    totals, squares = lax.psum(
        (jnp.sum(grouped, axis=(1, 2, 4)), jnp.sum(grouped * grouped, axis=(1, 2, 4))), "rows"
    )
    group_mean = totals / group_cells
    inv_std = lax.rsqrt(squares / group_cells - group_mean * group_mean + NORM_EPS)
    shaped = latents.astype(jnp.float32).reshape(images, -1, col_count, groups, CH_GROUP)
    norm_groups = (shaped - group_mean[:, None, None, :, None]) * inv_std[:, None, None, :, None]
    normalized = norm_groups.reshape(images, -1, col_count, channels)
    norm_groups, normalized, pre_act = (norm_groups, normalized, normalized * gn_gain + gn_bias)
    hidden = jax.nn.silu(pre_act).astype(jnp.bfloat16)
    grad_rim = None
    extended = with_rim(hidden)
    temb_features = jax.nn.silu(sinusoid(timesteps, temb_weight.shape[0])).astype(jnp.bfloat16)
    time_shift = jnp.dot(temb_features, temb_weight, preferred_element_type=jnp.float32)
    features = conv_taps(extended, conv_weight, slab_rows, col_count, False)
    features_out = (features + conv_bias + time_shift[:, None, None, :]).astype(jnp.bfloat16)
    grad_rim = with_rim(cotangent)
    hidden_grad = conv_taps(grad_rim, conv_weight, slab_rows, col_count, True)
    sigmoid_act = jax.nn.sigmoid(pre_act)
    act_grad = hidden_grad * sigmoid_act * (1.0 + pre_act * (1.0 - sigmoid_act))
    hat_groups = (act_grad * gn_gain).reshape(images, slab_rows, col_count, groups, CH_GROUP)
    chan_weighted = jnp.sum(act_grad * normalized, axis=(1, 2))
    chan_plain = jnp.sum(act_grad, axis=(1, 2))
    chan_output = jnp.sum(cotangent.astype(jnp.float32), axis=(1, 2))
    row_weighted, row_plain, row_output = lax.psum((chan_weighted, chan_plain, chan_output), "rows")
    first_sum = jnp.sum((row_plain * gn_gain).reshape(images, groups, CH_GROUP), axis=2)
    second_sum = jnp.sum((row_weighted * gn_gain).reshape(images, groups, CH_GROUP), axis=2)
    image_terms = jnp.stack(
        [jnp.sum(row_weighted, axis=0), jnp.sum(row_plain, axis=0), jnp.sum(row_output, axis=0)]
    )
    param_sums = lax.psum(image_terms, "dp")
    first_mean = first_sum / group_cells
    second_mean = second_sum / group_cells
    expand = (slice(None), None, None, slice(None), None)
    input_grad = inv_std[expand] * (
        hat_groups - first_mean[expand] - norm_groups * second_mean[expand]
    )
    input_grad = input_grad.reshape(images, slab_rows, col_count, channels).astype(jnp.bfloat16)
    grad_scale = 1.0 / math.sqrt(images * lax.axis_size("dp") * slab_rows * row_devices * col_count)
    return (features_out, input_grad, param_sums * grad_scale)


def solution(mesh):
    placed = (
        P("dp", "rows", None, None),
        P("dp"),
        P(),
        P(),
        P(),
        P(),
        P(),
        P("dp", "rows", None, None),
    )
    return jax.shard_map(
        per_device,
        mesh=mesh,
        in_specs=placed,
        out_specs=(P("dp", "rows", None, None), P("dp", "rows", None, None), P()),
        check_vma=False,
    )
```

profile of v0, /device:TPU:1, one launch (start us, length us, event | category | flops | bytes accessed | tf_op | source)
XLA Modules:
  0.0 90.6 jit_solution(9384634397204570961)
XLA Ops:
  0.7 1.2 %fusion.69 = (bf16[1,1,128,640]{3,2,1,0:T(8,128)(2,1)S(1)}, bf16[1,1,128,640]{3,2,1,0:T(8,128)(2,1)S(1)}) fusion(bf16[1,2,128,640]{3,2,1,0:T(8,128)(2,1)} %param.15), kind=kLoop, calls=%fused_computation.109 | loop fusion | bytes 655360 | tf_op jit(solution)/shard_map/slice | solution.py:16
  1.8 4.5 %collective-permute-start.2 = (bf16[1,1,128,640]{3,2,1,0:T(8,128)(2,1)S(1)}, bf16[1,1,128,640]{3,2,1,0:T(8,128)(2,1)S(1)}, u32[]{:S(2)}, u32[]{:S(2)}) collective-permute-start(bf16[1,1,128,640]{3,2,1,0:T(8,128)(2,1)S(1)} %get-tuple-element.30), channel_id=1, source_target_pairs={{0,8},{8,16},{16,24},{1,9},{9,17},{17,25},{2,10},{10,18},{18,26},{... | collective-permute-start | bytes 491528 | tf_op jit(solution)/shard_map/ppermute | solution.py:19
  6.3 1.9 %collective-permute-start.3 = (bf16[1,1,128,640]{3,2,1,0:T(8,128)(2,1)S(1)}, bf16[1,1,128,640]{3,2,1,0:T(8,128)(2,1)S(1)}, u32[]{:S(2)}, u32[]{:S(2)}) collective-permute-start(bf16[1,1,128,640]{3,2,1,0:T(8,128)(2,1)S(1)} %get-tuple-element.31), channel_id=1, source_target_pairs={{8,0},{16,8},{24,16},{9,1},{17,9},{25,17},{10,2},{18,10},{26,18},{... | collective-permute-start | bytes 491528 | tf_op jit(solution)/shard_map/ppermute | solution.py:21
  8.3 1.0 %convert_reduce_fusion.1 = f32[640]{0:T(1024)S(1)} fusion(bf16[1,2,128,640]{3,2,1,0:T(8,128)(2,1)} %param.15), kind=kLoop, calls=%fused_computation.87 | loop fusion | flops 327040 | bytes 330240 | tf_op jit(solution)/shard_map/reduce_sum | solution.py:99
  9.3 1.1 %convert_reduce_fusion = (f32[640]{0:T(1024)S(1)}, f32[640]{0:T(1024)S(1)}) fusion(bf16[1,2,128,640]{3,2,1,0:T(8,128)(2,1)} %param.8), kind=kLoop, calls=%fused_computation.22 | loop fusion | flops 654080 | bytes 332800 | tf_op jit(solution)/shard_map/reduce_sum | solution.py:77
  10.8 5.5 %all-reduce.3 = (f32[1,16]{1,0:T(1,128)S(1)}, f32[1,16]{1,0:T(1,128)S(1)}) all-reduce(f32[1,16]{1,0:T(1,128)S(1)} %bitcast.115, f32[1,16]{1,0:T(1,128)S(1)} %bitcast.114), channel_id=1, replica_groups=mesh['rows'=4,'dp'=8] {'rows'}, use_global_device_ids=true, to_apply=%region_5.6 | all-reduce | flops 32 | bytes 256 | tf_op jit(solution)/shard_map/psum | solution.py:76
  17.9 1.5 %select_maximum_fusion = bf16[1,4,130,640]{3,2,1,0:T(8,128)(2,1)S(1)} fusion(bf16[1,1,128,640]{3,2,1,0:T(8,128)(2,1)S(1)} %collective-permute-done.3, bf16[1,2,128,640]{3,2,1,0:T(8,128)(2,1)} %param.15, bf16[1,1,128,640]{3,2,1,0:T(8,128)(2,1)S(1)} %collective-permute-done.2), kind=kLoop, calls=%fused_computation.63 | loop fusion | flops 3993600 | bytes 1320960 | tf_op jit(solution)/shard_map/concatenate | solution.py:17
  19.6 1.6 %fusion.21 = f32[256,640]{1,0:T(8,128)S(1)} fusion(bf16[256,640]{1,0:T(8,128)(2,1)S(1)} %bitcast.112, bf16[3,3,640,640]{3,2,1,0:T(8,128)(2,1)} %param.12), kind=kOutput, calls=%fused_computation.41 | convolution fusion | flops 209715200 | bytes 1802240 | tf_op jit(solution)/shard_map/dot_general | solution.py:54
  22.8 0.5 convolution_add_fusion.4
  23.8 0.5 convolution_add_fusion.2
  24.2 0.5 convolution_add_fusion.1
  25.7 5.8 %all-reduce.2 = (f32[1,640]{1,0:T(1,128)S(1)}, f32[1,640]{1,0:T(1,128)S(1)}, f32[1,640]{1,0:T(1,128)S(1)}) all-reduce(f32[1,640]{1,0:T(1,128)S(1)} %reduce_sum.108, f32[1,640]{1,0:T(1,128)S(1)} %reduce_sum.111, f32[1,640]{1,0:T(1,128)S(1)} %reduce_sum.114), channel_id=1, replica_groups=mesh['rows'=4,'dp'=8] {'rows'}, use_global_device_ids=true, to_apply=%region_7.8 | all-reduce | flops 1920 | bytes 15360 | tf_op jit(solution)/shard_map/psum | solution.py:100
  31.5 30.2 %psum.47 = f32[3,640]{1,0:T(4,128)S(1)} all-reduce(f32[3,640]{1,0:T(4,128)S(1)} %pad_maximum_fusion.4), channel_id=1, replica_groups=mesh['rows'=4,'dp'=8] {'dp'}, use_global_device_ids=true, to_apply=%region_14.15 | all-reduce | flops 1920 | bytes 15360 | tf_op jit(solution)/shard_map/psum | solution.py:106
  62.6 11.1 %collective-permute-start = (bf16[1,1,128,640]{3,2,1,0:T(8,128)(2,1)S(1)}, bf16[1,1,128,640]{3,2,1,0:T(8,128)(2,1)S(1)}, u32[]{:S(2)}, u32[]{:S(2)}) collective-permute-start(bf16[1,1,128,640]{3,2,1,0:T(8,128)(2,1)S(1)} %get-tuple-element.34), channel_id=1, source_target_pairs={{0,8},{8,16},{16,24},{1,9},{9,17},{17,25},{2,10},{10,18},{18,26},{... | collective-permute-start | bytes 491528 | tf_op jit(solution)/shard_map/ppermute | solution.py:19
  73.7 1.9 %collective-permute-start.1 = (bf16[1,1,128,640]{3,2,1,0:T(8,128)(2,1)S(1)}, bf16[1,1,128,640]{3,2,1,0:T(8,128)(2,1)S(1)}, u32[]{:S(2)}, u32[]{:S(2)}) collective-permute-start(bf16[1,1,128,640]{3,2,1,0:T(8,128)(2,1)S(1)} %get-tuple-element.35), channel_id=1, source_target_pairs={{8,0},{16,8},{24,16},{9,1},{17,9},{25,17},{10,2},{18,10},{26,18},{... | collective-permute-start | bytes 491528 | tf_op jit(solution)/shard_map/ppermute | solution.py:21
  75.6 0.9 %fusion.61 = bf16[1,2,128,640]{3,2,1,0:T(8,128)(2,1)} fusion(bf16[1,2,128,640]{3,2,1,0:T(8,128)(2,1)S(1)} %copy-done.3, f32[1,2,128,640]{3,2,1,0:T(8,128)S(1)} %get-tuple-element.14, f32[640]{0:T(1024)S(1)} %mul.180, f32[640]{0:T(1024)S(1)} %sub.67, f32[640]{0:T(1024)S(1)} %copy-done.4, f32[640]{0:T(1024)S(1)} %mul.162, f32[640]{0:T(1024)S(1)} %sub.61), kind=kLoop, calls=%fused_computation.85 | loop fusion | flops 1474560 | bytes 1323520 | tf_op jit(solution)/shard_map/convert_element_type | solution.py:113
  76.5 0.6 broadcast_multiply_fusion
  77.1 3.2 %collective-permute-done.1 = bf16[1,1,128,640]{3,2,1,0:T(8,128)(2,1)S(1)} collective-permute-done((bf16[1,1,128,640]{3,2,1,0:T(8,128)(2,1)S(1)}, bf16[1,1,128,640]{3,2,1,0:T(8,128)(2,1)S(1)}, u32[]{:S(2)}, u32[]{:S(2)}) %collective-permute-start.1) | collective-permute-done | bytes 163872 | tf_op jit(solution)/shard_map/ppermute | solution.py:21
  80.8 1.6 %fusion.23 = f32[256,640]{1,0:T(8,128)S(1)} fusion(bf16[256,640]{1,0:T(8,128)(2,1)S(1)} %bitcast.113, bf16[3,3,640,640]{3,2,1,0:T(8,128)(2,1)} %param.12), kind=kOutput, calls=%fused_computation.43 | convolution fusion | flops 209715200 | bytes 1802240 | tf_op jit(solution)/shard_map/dot_general | solution.py:61
  82.4 1.8 %fusion.5 = f32[256,640]{1,0:T(8,128)S(1)} fusion(bf16[256,640]{1,0:T(8,128)(2,1)S(1)} %bitcast.111, bf16[3,3,640,640]{3,2,1,0:T(8,128)(2,1)} %param.12), kind=kOutput, calls=%fused_computation.25 | convolution fusion | flops 209715200 | bytes 1802240 | tf_op jit(solution)/shard_map/dot_general | solution.py:61
  84.2 1.6 %convolution_add_fusion.13 = f32[256,640]{1,0:T(8,128)S(1)} fusion(f32[256,640]{1,0:T(8,128)S(1)} %fusion.23, bf16[256,640]{1,0:T(8,128)(2,1)S(1)} %bitcast.101, bf16[3,3,640,640]{3,2,1,0:T(8,128)(2,1)} %param.12), kind=kOutput, calls=%fused_computation.16 | convolution fusion | flops 209879040 | bytes 2457600 | tf_op jit(solution)/shard_map/dot_general | solution.py:61
  85.9 1.6 %convolution_add_fusion.12 = f32[256,640]{1,0:T(8,128)S(1)} fusion(f32[256,640]{1,0:T(8,128)S(1)} %convolution_add_fusion.13, bf16[256,640]{1,0:T(8,128)(2,1)S(1)} %bitcast.109, bf16[3,3,640,640]{3,2,1,0:T(8,128)(2,1)} %param.12), kind=kOutput, calls=%fused_computation.15 | convolution fusion | flops 209879040 | bytes 2457600 | tf_op jit(solution)/shard_map/dot_general | solution.py:61
  89.4 0.5 fusion.1
  89.8 0.8 add_convert_fusion
  (66 shorter events, 7.4 us)
Async XLA Ops:
  0.6 16.9 %copy-start = (bf16[1280,640]{1,0:T(8,128)(2,1)S(1)}, bf16[1280,640]{1,0:T(8,128)(2,1)}, u32[]{:S(2)}) copy-start(bf16[1280,640]{1,0:T(8,128)(2,1)} %param.14) | copy-start | bytes 4915204
  0.6 21.1 %copy-start.2 = (bf16[1,2,128,640]{3,2,1,0:T(8,128)(2,1)S(1)}, bf16[1,2,128,640]{3,2,1,0:T(8,128)(2,1)}, u32[]{:S(2)}) copy-start(bf16[1,2,128,640]{3,2,1,0:T(8,128)(2,1)} %param.15) | copy-start | bytes 983044
  1.8 16.1 %collective-permute-start.2 = (bf16[1,1,128,640]{3,2,1,0:T(8,128)(2,1)S(1)}, bf16[1,1,128,640]{3,2,1,0:T(8,128)(2,1)S(1)}, u32[]{:S(2)}, u32[]{:S(2)}) collective-permute-start(bf16[1,1,128,640]{3,2,1,0:T(8,128)(2,1)S(1)} %get-tuple-element.30), channel_id=1, source_target_pairs={{0,8},{8,16},{16,24},{1,9},{9,17},{17,25},{2,10},{10,18},{18,26},{... | collective-permute-start | bytes 491528 | tf_op jit(solution)/shard_map/ppermute | solution.py:19
  6.3 11.6 %collective-permute-start.3 = (bf16[1,1,128,640]{3,2,1,0:T(8,128)(2,1)S(1)}, bf16[1,1,128,640]{3,2,1,0:T(8,128)(2,1)S(1)}, u32[]{:S(2)}, u32[]{:S(2)}) collective-permute-start(bf16[1,1,128,640]{3,2,1,0:T(8,128)(2,1)S(1)} %get-tuple-element.31), channel_id=1, source_target_pairs={{8,0},{16,8},{24,16},{9,1},{17,9},{25,17},{10,2},{18,10},{26,18},{... | collective-permute-start | bytes 491528 | tf_op jit(solution)/shard_map/ppermute | solution.py:21
  16.6 4.6 %copy-start.1 = (bf16[3,3,640,640]{3,2,1,0:T(8,128)(2,1)S(1)}, bf16[3,3,640,640]{3,2,1,0:T(8,128)(2,1)}, u32[]{:S(2)}) copy-start(bf16[3,3,640,640]{3,2,1,0:T(8,128)(2,1)} %param.12) | copy-start | bytes 22118404
  22.3 2.9 %copy-start.3 = (bf16[1,2,128,640]{3,2,1,0:T(8,128)(2,1)S(1)}, bf16[1,2,128,640]{3,2,1,0:T(8,128)(2,1)}, u32[]{:S(2)}) copy-start(bf16[1,2,128,640]{3,2,1,0:T(8,128)(2,1)} %param.8) | copy-start | bytes 983044
  22.3 2.9 %copy-start.4 = (f32[640]{0:T(1024)S(1)}, f32[640]{0:T(1024)}, u32[]{:S(2)}) copy-start(f32[640]{0:T(1024)} %param.10) | copy-start | bytes 7684
  22.3 2.9 %copy-start.5 = (f32[640]{0:T(1024)S(1)}, f32[640]{0:T(1024)}, u32[]{:S(2)}) copy-start(f32[640]{0:T(1024)} %param.11) | copy-start | bytes 7684
  62.6 14.6 %collective-permute-start = (bf16[1,1,128,640]{3,2,1,0:T(8,128)(2,1)S(1)}, bf16[1,1,128,640]{3,2,1,0:T(8,128)(2,1)S(1)}, u32[]{:S(2)}, u32[]{:S(2)}) collective-permute-start(bf16[1,1,128,640]{3,2,1,0:T(8,128)(2,1)S(1)} %get-tuple-element.34), channel_id=1, source_target_pairs={{0,8},{8,16},{16,24},{1,9},{9,17},{17,25},{2,10},{10,18},{18,26},{... | collective-permute-start | bytes 491528 | tf_op jit(solution)/shard_map/ppermute | solution.py:19
  73.7 6.6 %collective-permute-start.1 = (bf16[1,1,128,640]{3,2,1,0:T(8,128)(2,1)S(1)}, bf16[1,1,128,640]{3,2,1,0:T(8,128)(2,1)S(1)}, u32[]{:S(2)}, u32[]{:S(2)}) collective-permute-start(bf16[1,1,128,640]{3,2,1,0:T(8,128)(2,1)S(1)} %get-tuple-element.35), channel_id=1, source_target_pairs={{8,0},{16,8},{24,16},{9,1},{17,9},{25,17},{10,2},{18,10},{26,18},{... | collective-permute-start | bytes 491528 | tf_op jit(solution)/shard_map/ppermute | solution.py:21
  77.1 10.4 %slice-start = ((s8[7372800]{0:T(1024)(128)(4,1)}), s8[3178496]{0:T(1024)(128)(4,1)S(1)}, s32[]{:S(2)}) async-start(s8[7372800]{0:T(1024)(128)(4,1)} %bitcast.93), calls=%async_computation | async-start | bytes 6356992
  82.4 5.1 %slice-start.1 = ((s8[7372800]{0:T(1024)(128)(4,1)}), s8[4194304]{0:T(1024)(128)(4,1)S(1)}, s32[]{:S(2)}) async-start(s8[7372800]{0:T(1024)(128)(4,1)} %bitcast.93), calls=%async_computation.1 | async-start | bytes 8388608
  85.8 4.0 %copy-start.6 = (f32[640]{0:T(1024)S(1)}, f32[640]{0:T(1024)}, u32[]{:S(2)}) copy-start(f32[640]{0:T(1024)} %param.13) | copy-start | bytes 7684
where the time goes:
time: 91.1 us; the launch traced here: 90.6 us
  blocking collectives  41.6 us (46%)
  starting transfers between devices  19.4 us (21%)
  matrix products  14.6 us (16%)
  other arithmetic  7.23 us (8%)
  waiting for transfers between devices  3.2 us (4%)
  local copies, waits for them, and re-layouts  2.72 us (3%)
  between operations  1.93 us (2%)
    psum x1, blocking collectives, per_device(): param_sums = lax.psum(image_terms, 'dp')  30.2 us
    ppermute x2, starting transfers between devices, padded_2(): lax.ppermute(tail, axis, [(i, (i + 1) % count) for i in range(ends)])  15.6 us
    dot_general x9, matrix products, conv_taps(): jnp.dot(window, weight[tap_row, tap_col], preferred_element_type=jnp.floa...  8.88 us
    psum x1, blocking collectives, per_device(): lax.psum((chan_weighted, chan_plain, chan_output), 'rows')  5.81 us
    psum x1, blocking collectives, per_device(): lax.psum((jnp.sum(grouped, axis=(1, 2, 4)), jnp.sum(grouped * grouped, ax...  5.51 us
    dot_general x9, matrix products, conv_taps(): lax.dot_general(window, weight[tap_row, tap_col], (((1,), (1,)), ((), ())...  5.35 us
    ppermute x2, starting transfers between devices, padded_2(): lax.ppermute(head, axis, [((i + 1) % count, i) for i in range(ends)])  3.84 us
    ppermute x2, waiting for transfers between devices, padded_2(): lax.ppermute(head, axis, [((i + 1) % count, i) for i in range(ends)])  3.19 us
  transfers between devices with their start and end apart: 4, of which 1 were waited for; matrix products, arithmetic and copies ran while one was open for 5% of the time, Pallas kernels for 0%

commit v1 on v0

--- a/solution.py
+++ b/solution.py
@@ -103,7 +103,8 @@
     image_terms = jnp.stack(
         [jnp.sum(row_weighted, axis=0), jnp.sum(row_plain, axis=0), jnp.sum(row_output, axis=0)]
     )
-    param_sums = lax.psum(image_terms, "dp")
+    parts = lax.all_gather(image_terms, "dp", axis=0, tiled=False)
+    param_sums = parts.sum(axis=0)
     first_mean = first_sum / group_cells
     second_mean = second_sum / group_cells
     expand = (slice(None), None, None, slice(None), None)

time: 91.1 us -> 84.6 us (0.929)
  blocking collectives: 41.6 us -> 36 us
    psum x1 -> x0, blocking collectives: 30.2 us -> none  [per_device(): param_sums = lax.psum(image_terms, 'dp')]
    all_gather x0 -> x1, blocking collectives: none -> 24.7 us  [per_device(): parts = lax.all_gather(image_terms, 'dp', axis=0, tiled=False)]
    ppermute x2, starting transfers between devices: 15.6 us -> 14.6 us  [padded_2(): lax.ppermute(tail, axis, [(i, (i + 1) % count) for i in range(ends)])]
  transfers between devices with their start and end apart: 4 -> 4, of which waited for: 1 -> 1; matrix products, arithmetic and copies ran while one was open for 5% -> 6% of each run, Pallas kernels for 0% -> 0%
where the time goes in v1:
time: 84.6 us; the launch traced here: 84.1 us
  blocking collectives  36 us (43%)
  starting transfers between devices  18.5 us (22%)
  matrix products  14.6 us (17%)
  other arithmetic  7.25 us (9%)
  waiting for transfers between devices  3.2 us (4%)
  local copies, waits for them, and re-layouts  2.73 us (3%)
  between operations  1.93 us (2%)
    all_gather x1, blocking collectives, per_device(): parts = lax.all_gather(image_terms, 'dp', axis=0, tiled=False)  24.7 us
    ppermute x2, starting transfers between devices, padded_2(): lax.ppermute(tail, axis, [(i, (i + 1) % count) for i in range(ends)])  14.6 us
    dot_general x9, matrix products, conv_taps(): jnp.dot(window, weight[tap_row, tap_col], preferred_element_type=jnp.floa...  8.88 us
    psum x1, blocking collectives, per_device(): lax.psum((chan_weighted, chan_plain, chan_output), 'rows')  5.81 us
    psum x1, blocking collectives, per_device(): lax.psum((jnp.sum(grouped, axis=(1, 2, 4)), jnp.sum(grouped * grouped, ax...  5.51 us
    dot_general x9, matrix products, conv_taps(): lax.dot_general(window, weight[tap_row, tap_col], (((1,), (1,)), ((), ())...  5.35 us
    ppermute x2, starting transfers between devices, padded_2(): lax.ppermute(head, axis, [((i + 1) % count, i) for i in range(ends)])  3.84 us
    ppermute x2, waiting for transfers between devices, padded_2(): lax.ppermute(head, axis, [((i + 1) % count, i) for i in range(ends)])  3.19 us
  transfers between devices with their start and end apart: 4, of which 1 were waited for; matrix products, arithmetic and copies ran while one was open for 6% of the time, Pallas kernels for 0%

profile of v1, /device:TPU:1, one launch (start us, length us, event | category | flops | bytes accessed | tf_op | source)
XLA Modules:
  0.0 84.1 jit_solution(1156609977914487084)
XLA Ops:
  0.7 1.2 %fusion.69 = (bf16[1,1,128,640]{3,2,1,0:T(8,128)(2,1)S(1)}, bf16[1,1,128,640]{3,2,1,0:T(8,128)(2,1)S(1)}) fusion(bf16[1,2,128,640]{3,2,1,0:T(8,128)(2,1)} %param.15), kind=kLoop, calls=%fused_computation.109 | loop fusion | bytes 655360 | tf_op jit(solution)/shard_map/slice | solution.py:16
  1.8 4.5 %collective-permute-start.2 = (bf16[1,1,128,640]{3,2,1,0:T(8,128)(2,1)S(1)}, bf16[1,1,128,640]{3,2,1,0:T(8,128)(2,1)S(1)}, u32[]{:S(2)}, u32[]{:S(2)}) collective-permute-start(bf16[1,1,128,640]{3,2,1,0:T(8,128)(2,1)S(1)} %get-tuple-element.30), channel_id=1, source_target_pairs={{0,8},{8,16},{16,24},{1,9},{9,17},{17,25},{2,10},{10,18},{18,26},{... | collective-permute-start | bytes 491528 | tf_op jit(solution)/shard_map/ppermute | solution.py:19
  6.3 1.9 %collective-permute-start.3 = (bf16[1,1,128,640]{3,2,1,0:T(8,128)(2,1)S(1)}, bf16[1,1,128,640]{3,2,1,0:T(8,128)(2,1)S(1)}, u32[]{:S(2)}, u32[]{:S(2)}) collective-permute-start(bf16[1,1,128,640]{3,2,1,0:T(8,128)(2,1)S(1)} %get-tuple-element.31), channel_id=1, source_target_pairs={{8,0},{16,8},{24,16},{9,1},{17,9},{25,17},{10,2},{18,10},{26,18},{... | collective-permute-start | bytes 491528 | tf_op jit(solution)/shard_map/ppermute | solution.py:21
  8.3 1.0 %convert_reduce_fusion.1 = f32[640]{0:T(1024)S(1)} fusion(bf16[1,2,128,640]{3,2,1,0:T(8,128)(2,1)} %param.15), kind=kLoop, calls=%fused_computation.87 | loop fusion | flops 327040 | bytes 330240 | tf_op jit(solution)/shard_map/reduce_sum | solution.py:99
  9.3 1.1 %convert_reduce_fusion = (f32[640]{0:T(1024)S(1)}, f32[640]{0:T(1024)S(1)}) fusion(bf16[1,2,128,640]{3,2,1,0:T(8,128)(2,1)} %param.8), kind=kLoop, calls=%fused_computation.22 | loop fusion | flops 654080 | bytes 332800 | tf_op jit(solution)/shard_map/reduce_sum | solution.py:77
  10.8 5.5 %all-reduce.3 = (f32[1,16]{1,0:T(1,128)S(1)}, f32[1,16]{1,0:T(1,128)S(1)}) all-reduce(f32[1,16]{1,0:T(1,128)S(1)} %bitcast.117, f32[1,16]{1,0:T(1,128)S(1)} %bitcast.116), channel_id=1, replica_groups=mesh['rows'=4,'dp'=8] {'rows'}, use_global_device_ids=true, to_apply=%region_5.6 | all-reduce | flops 32 | bytes 256 | tf_op jit(solution)/shard_map/psum | solution.py:76
  17.9 1.5 %select_maximum_fusion = bf16[1,4,130,640]{3,2,1,0:T(8,128)(2,1)S(1)} fusion(bf16[1,1,128,640]{3,2,1,0:T(8,128)(2,1)S(1)} %collective-permute-done.3, bf16[1,2,128,640]{3,2,1,0:T(8,128)(2,1)} %param.15, bf16[1,1,128,640]{3,2,1,0:T(8,128)(2,1)S(1)} %collective-permute-done.2), kind=kLoop, calls=%fused_computation.63 | loop fusion | flops 3993600 | bytes 1320960 | tf_op jit(solution)/shard_map/concatenate | solution.py:17
  19.6 1.6 %fusion.21 = f32[256,640]{1,0:T(8,128)S(1)} fusion(bf16[256,640]{1,0:T(8,128)(2,1)S(1)} %bitcast.114, bf16[3,3,640,640]{3,2,1,0:T(8,128)(2,1)} %param.12), kind=kOutput, calls=%fused_computation.41 | convolution fusion | flops 209715200 | bytes 1802240 | tf_op jit(solution)/shard_map/dot_general | solution.py:54
  22.8 0.5 convolution_add_fusion.4
  23.8 0.5 convolution_add_fusion.2
  24.2 0.5 convolution_add_fusion.1
  25.7 5.8 %all-reduce.2 = (f32[1,640]{1,0:T(1,128)S(1)}, f32[1,640]{1,0:T(1,128)S(1)}, f32[1,640]{1,0:T(1,128)S(1)}) all-reduce(f32[1,640]{1,0:T(1,128)S(1)} %reduce_sum.117, f32[1,640]{1,0:T(1,128)S(1)} %reduce_sum.120, f32[1,640]{1,0:T(1,128)S(1)} %reduce_sum.123), channel_id=1, replica_groups=mesh['rows'=4,'dp'=8] {'rows'}, use_global_device_ids=true, to_apply=%region_7.8 | all-reduce | flops 1920 | bytes 15360 | tf_op jit(solution)/shard_map/psum | solution.py:100
  31.5 24.7 %all-gather.1 = f32[8,3,640]{2,1,0:T(4,128)S(1)} all-gather(f32[1,3,640]{2,1,0:T(4,128)S(1)} %maximum_bitcast_fusion), channel_id=2, replica_groups=mesh['rows'=4,'dp'=8] {'dp'}, dimensions={0}, use_global_device_ids=true | all-gather | bytes 69120 | tf_op jit(solution)/shard_map/all_gather | solution.py:106
  57.0 10.1 %collective-permute-start = (bf16[1,1,128,640]{3,2,1,0:T(8,128)(2,1)S(1)}, bf16[1,1,128,640]{3,2,1,0:T(8,128)(2,1)S(1)}, u32[]{:S(2)}, u32[]{:S(2)}) collective-permute-start(bf16[1,1,128,640]{3,2,1,0:T(8,128)(2,1)S(1)} %get-tuple-element.34), channel_id=1, source_target_pairs={{0,8},{8,16},{16,24},{1,9},{9,17},{17,25},{2,10},{10,18},{18,26},{... | collective-permute-start | bytes 491528 | tf_op jit(solution)/shard_map/ppermute | solution.py:19
  67.2 1.9 %collective-permute-start.1 = (bf16[1,1,128,640]{3,2,1,0:T(8,128)(2,1)S(1)}, bf16[1,1,128,640]{3,2,1,0:T(8,128)(2,1)S(1)}, u32[]{:S(2)}, u32[]{:S(2)}) collective-permute-start(bf16[1,1,128,640]{3,2,1,0:T(8,128)(2,1)S(1)} %get-tuple-element.35), channel_id=1, source_target_pairs={{8,0},{16,8},{24,16},{9,1},{17,9},{25,17},{10,2},{18,10},{26,18},{... | collective-permute-start | bytes 491528 | tf_op jit(solution)/shard_map/ppermute | solution.py:21
  69.1 0.9 %fusion.61 = bf16[1,2,128,640]{3,2,1,0:T(8,128)(2,1)} fusion(bf16[1,2,128,640]{3,2,1,0:T(8,128)(2,1)S(1)} %copy-done.3, f32[1,2,128,640]{3,2,1,0:T(8,128)S(1)} %get-tuple-element.14, f32[640]{0:T(1024)S(1)} %mul.180, f32[640]{0:T(1024)S(1)} %sub.67, f32[640]{0:T(1024)S(1)} %copy-done.4, f32[640]{0:T(1024)S(1)} %mul.162, f32[640]{0:T(1024)S(1)} %sub.61), kind=kLoop, calls=%fused_computation.85 | loop fusion | flops 1474560 | bytes 1323520 | tf_op jit(solution)/shard_map/convert_element_type | solution.py:114
  70.0 0.6 broadcast_multiply_fusion
  70.6 3.2 %collective-permute-done.1 = bf16[1,1,128,640]{3,2,1,0:T(8,128)(2,1)S(1)} collective-permute-done((bf16[1,1,128,640]{3,2,1,0:T(8,128)(2,1)S(1)}, bf16[1,1,128,640]{3,2,1,0:T(8,128)(2,1)S(1)}, u32[]{:S(2)}, u32[]{:S(2)}) %collective-permute-start.1) | collective-permute-done | bytes 163872 | tf_op jit(solution)/shard_map/ppermute | solution.py:21
  74.3 1.6 %fusion.23 = f32[256,640]{1,0:T(8,128)S(1)} fusion(bf16[256,640]{1,0:T(8,128)(2,1)S(1)} %bitcast.115, bf16[3,3,640,640]{3,2,1,0:T(8,128)(2,1)} %param.12), kind=kOutput, calls=%fused_computation.43 | convolution fusion | flops 209715200 | bytes 1802240 | tf_op jit(solution)/shard_map/dot_general | solution.py:61
  75.9 1.8 %fusion.5 = f32[256,640]{1,0:T(8,128)S(1)} fusion(bf16[256,640]{1,0:T(8,128)(2,1)S(1)} %bitcast.113, bf16[3,3,640,640]{3,2,1,0:T(8,128)(2,1)} %param.12), kind=kOutput, calls=%fused_computation.25 | convolution fusion | flops 209715200 | bytes 1802240 | tf_op jit(solution)/shard_map/dot_general | solution.py:61
  77.7 1.6 %convolution_add_fusion.13 = f32[256,640]{1,0:T(8,128)S(1)} fusion(f32[256,640]{1,0:T(8,128)S(1)} %fusion.23, bf16[256,640]{1,0:T(8,128)(2,1)S(1)} %bitcast.103, bf16[3,3,640,640]{3,2,1,0:T(8,128)(2,1)} %param.12), kind=kOutput, calls=%fused_computation.16 | convolution fusion | flops 209879040 | bytes 2457600 | tf_op jit(solution)/shard_map/dot_general | solution.py:61
  79.4 1.6 %convolution_add_fusion.12 = f32[256,640]{1,0:T(8,128)S(1)} fusion(f32[256,640]{1,0:T(8,128)S(1)} %convolution_add_fusion.13, bf16[256,640]{1,0:T(8,128)(2,1)S(1)} %bitcast.111, bf16[3,3,640,640]{3,2,1,0:T(8,128)(2,1)} %param.12), kind=kOutput, calls=%fused_computation.15 | convolution fusion | flops 209879040 | bytes 2457600 | tf_op jit(solution)/shard_map/dot_general | solution.py:61
  82.9 0.5 fusion.1
  83.4 0.8 add_convert_fusion
  (67 shorter events, 7.4 us)
Async XLA Ops:
  0.6 16.9 %copy-start = (bf16[1280,640]{1,0:T(8,128)(2,1)S(1)}, bf16[1280,640]{1,0:T(8,128)(2,1)}, u32[]{:S(2)}) copy-start(bf16[1280,640]{1,0:T(8,128)(2,1)} %param.14) | copy-start | bytes 4915204
  0.6 21.1 %copy-start.2 = (bf16[1,2,128,640]{3,2,1,0:T(8,128)(2,1)S(1)}, bf16[1,2,128,640]{3,2,1,0:T(8,128)(2,1)}, u32[]{:S(2)}) copy-start(bf16[1,2,128,640]{3,2,1,0:T(8,128)(2,1)} %param.15) | copy-start | bytes 983044
  1.8 16.1 %collective-permute-start.2 = (bf16[1,1,128,640]{3,2,1,0:T(8,128)(2,1)S(1)}, bf16[1,1,128,640]{3,2,1,0:T(8,128)(2,1)S(1)}, u32[]{:S(2)}, u32[]{:S(2)}) collective-permute-start(bf16[1,1,128,640]{3,2,1,0:T(8,128)(2,1)S(1)} %get-tuple-element.30), channel_id=1, source_target_pairs={{0,8},{8,16},{16,24},{1,9},{9,17},{17,25},{2,10},{10,18},{18,26},{... | collective-permute-start | bytes 491528 | tf_op jit(solution)/shard_map/ppermute | solution.py:19
  6.3 11.6 %collective-permute-start.3 = (bf16[1,1,128,640]{3,2,1,0:T(8,128)(2,1)S(1)}, bf16[1,1,128,640]{3,2,1,0:T(8,128)(2,1)S(1)}, u32[]{:S(2)}, u32[]{:S(2)}) collective-permute-start(bf16[1,1,128,640]{3,2,1,0:T(8,128)(2,1)S(1)} %get-tuple-element.31), channel_id=1, source_target_pairs={{8,0},{16,8},{24,16},{9,1},{17,9},{25,17},{10,2},{18,10},{26,18},{... | collective-permute-start | bytes 491528 | tf_op jit(solution)/shard_map/ppermute | solution.py:21
  16.6 4.6 %copy-start.1 = (bf16[3,3,640,640]{3,2,1,0:T(8,128)(2,1)S(1)}, bf16[3,3,640,640]{3,2,1,0:T(8,128)(2,1)}, u32[]{:S(2)}) copy-start(bf16[3,3,640,640]{3,2,1,0:T(8,128)(2,1)} %param.12) | copy-start | bytes 22118404
  22.3 2.9 %copy-start.3 = (bf16[1,2,128,640]{3,2,1,0:T(8,128)(2,1)S(1)}, bf16[1,2,128,640]{3,2,1,0:T(8,128)(2,1)}, u32[]{:S(2)}) copy-start(bf16[1,2,128,640]{3,2,1,0:T(8,128)(2,1)} %param.8) | copy-start | bytes 983044
  22.3 2.9 %copy-start.4 = (f32[640]{0:T(1024)S(1)}, f32[640]{0:T(1024)}, u32[]{:S(2)}) copy-start(f32[640]{0:T(1024)} %param.10) | copy-start | bytes 7684
  22.3 2.9 %copy-start.5 = (f32[640]{0:T(1024)S(1)}, f32[640]{0:T(1024)}, u32[]{:S(2)}) copy-start(f32[640]{0:T(1024)} %param.11) | copy-start | bytes 7684
  57.0 13.6 %collective-permute-start = (bf16[1,1,128,640]{3,2,1,0:T(8,128)(2,1)S(1)}, bf16[1,1,128,640]{3,2,1,0:T(8,128)(2,1)S(1)}, u32[]{:S(2)}, u32[]{:S(2)}) collective-permute-start(bf16[1,1,128,640]{3,2,1,0:T(8,128)(2,1)S(1)} %get-tuple-element.34), channel_id=1, source_target_pairs={{0,8},{8,16},{16,24},{1,9},{9,17},{17,25},{2,10},{10,18},{18,26},{... | collective-permute-start | bytes 491528 | tf_op jit(solution)/shard_map/ppermute | solution.py:19
  67.2 6.6 %collective-permute-start.1 = (bf16[1,1,128,640]{3,2,1,0:T(8,128)(2,1)S(1)}, bf16[1,1,128,640]{3,2,1,0:T(8,128)(2,1)S(1)}, u32[]{:S(2)}, u32[]{:S(2)}) collective-permute-start(bf16[1,1,128,640]{3,2,1,0:T(8,128)(2,1)S(1)} %get-tuple-element.35), channel_id=1, source_target_pairs={{8,0},{16,8},{24,16},{9,1},{17,9},{25,17},{10,2},{18,10},{26,18},{... | collective-permute-start | bytes 491528 | tf_op jit(solution)/shard_map/ppermute | solution.py:21
  70.6 10.4 %slice-start = ((s8[7372800]{0:T(1024)(128)(4,1)}), s8[3178496]{0:T(1024)(128)(4,1)S(1)}, s32[]{:S(2)}) async-start(s8[7372800]{0:T(1024)(128)(4,1)} %bitcast.95), calls=%async_computation | async-start | bytes 6356992
  75.9 5.1 %slice-start.1 = ((s8[7372800]{0:T(1024)(128)(4,1)}), s8[4194304]{0:T(1024)(128)(4,1)S(1)}, s32[]{:S(2)}) async-start(s8[7372800]{0:T(1024)(128)(4,1)} %bitcast.95), calls=%async_computation.1 | async-start | bytes 8388608
  79.4 4.0 %copy-start.6 = (f32[640]{0:T(1024)S(1)}, f32[640]{0:T(1024)}, u32[]{:S(2)}) copy-start(f32[640]{0:T(1024)} %param.13) | copy-start | bytes 7684
